TPU v7x, 256 devices: a whole 4x4x8 slice. The times are simulated.
256 devices in a mesh: dp: 32 (over x_lo, z, core), tensor: 8 (over x_hi, y).
Axes of the slice: x: 4 (x_hi: 2, x_lo: 2; x = x_hi * 2 + x_lo), y: 4, z: 8, core: 2. Of those that a mesh axis runs over, the one named last changes fastest.
Arguments:
- hidden_input_state: bfloat16 [12288, 4608], P('dp', 'tensor'), may hold values from -80 to 80
- norm_gain: float32 [4608], replicated, may hold values from 0.5 to 1.5
- head_weight: bfloat16 [4608, 8192], P(None, 'tensor'), may hold values from -2 to 2
- target_ids: int32 [12288], P('dp'), may hold values from 0 to 8191
Outputs:
- hidden_state_gradient: float32 [12288, 4608], P('dp', 'tensor')
- grad_head: float32 [4608, 8192], P('dp', 'tensor')
- norm_gain_gradient: float32 [4608], P('tensor')
All inputs are finite; a program needn't handle non-finite values.
Results may differ from a plain program's by a relative error of at most 0.0039.
Values may be sent and summed in bfloat16 or wider, within the bound.
No kernel may reach another device: no remote copies, remote signals or barrier semaphores. Data moves between devices by JAX's collectives and lax.ppermute only.
A program may use at most 192 MiB of HBM per device.

v0:
```python
import jax
import jax.numpy as jnp
from jax import lax
from jax.sharding import PartitionSpec as P

epsilon = 1e-06


def shards(hidden_input_state, norm_gain, head_weight, target_ids):
    local_cols = hidden_input_state.shape[1]
    vocab_rows = head_weight.shape[1]
    width = head_weight.shape[0]
    gathered = lax.all_gather(hidden_input_state, "tensor", axis=1, tiled=True)
    values = gathered.astype(jnp.float32)
    scaled_rows = lax.rsqrt(jnp.mean(values * values, axis=1, keepdims=True) + epsilon)
    normed = (values * scaled_rows * norm_gain[None, :]).astype(jnp.bfloat16)
    logits = jnp.dot(normed, head_weight, preferred_element_type=jnp.float32)
    local_top = jnp.max(logits, axis=1)
    local_total = jnp.sum(jnp.exp(logits - local_top[:, None]), axis=1)
    row_top = lax.pmax(local_top, "tensor")
    row_total = lax.psum(local_total * jnp.exp(local_top - row_top), "tensor")
    log_total = row_top + jnp.log(row_total)
    offset = lax.axis_index("tensor") * vocab_rows
    column_ids = offset + lax.broadcasted_iota(jnp.int32, (1, vocab_rows), 1)
    onehot = (column_ids == target_ids[:, None]).astype(jnp.float32)
    dlogits = (jnp.exp(logits - log_total[:, None]) - onehot).astype(jnp.bfloat16)
    start_col = lax.axis_index("tensor") * local_cols
    normalized_slice = hidden_input_state.astype(jnp.float32) * scaled_rows
    gain_slice = lax.dynamic_slice_in_dim(norm_gain, start_col, local_cols)
    grad_cols = lax.psum_scatter(
        lax.dot_general(
            head_weight, dlogits, (((1,), (1,)), ((), ())), preferred_element_type=jnp.float32
        ),
        "tensor",
        scatter_dimension=0,
        tiled=True,
    )
    normed_gradient = grad_cols.T
    partial_inner_sum = jnp.sum(normed_gradient * gain_slice[None, :] * normalized_slice, axis=1)
    row_inner_sum = lax.psum(partial_inner_sum, "tensor") / width
    weighted_rows = normed_gradient * gain_slice[None, :]
    hidden_state_gradient = scaled_rows * (
        weighted_rows - normalized_slice * row_inner_sum[:, None]
    )
    norm_gain_gradient = lax.psum(jnp.sum(normed_gradient * normalized_slice, axis=0), "dp")
    grad_head = lax.psum_scatter(
        lax.dot_general(
            normed, dlogits, (((0,), (0,)), ((), ())), preferred_element_type=jnp.float32
        ),
        "dp",
        scatter_dimension=0,
        tiled=True,
    )
    return (hidden_state_gradient, grad_head, norm_gain_gradient)


def solution(mesh):
    return jax.shard_map(
        shards,
        mesh=mesh,
        in_specs=(P("dp", "tensor"), P(), P(None, "tensor"), P("dp")),
        out_specs=(P("dp", "tensor"), P("dp", "tensor"), P("tensor")),
        check_vma=False,
    )
```

profile of v0, /device:TPU:1, one launch (start us, length us, event | category | flops | bytes accessed | tf_op | source)
XLA Modules:
  0.0 421.5 jit_solution(17505398155015696289)
XLA Ops:
  7.2 0.7 all-gather.2.cloned.1.call-update
  8.0 77.0 %all-gather.2.cloned.1.call-done = bf16[384,4608]{0,1:T(8,128)(2,1)} async-done(((bf16[384,576]{0,1:T(8,128)(2,1)}), bf16[384,4608]{0,1:T(8,128)(2,1)}) %all-gather.2.cloned.1.call-update) | async-done | bytes 3538960 | tf_op jit(solution)/shard_map/all_gather | solution.py:13
  85.0 3.0 fusion
  88.1 8.8 %fusion.8 = (f32[384]{0:T(512)S(1)}, f32[384,1024]{1,0:T(8,128)}) fusion(bf16[4608,1024]{1,0:T(8,128)(2,1)} %param.6, bf16[384,4608]{0,1:T(8,128)(2,1)S(1)} %copy-done, f32[4608]{0:T(1024)} %param.5, f32[384]{0:T(512)S(1)} %add_rsqrt_fusion), kind=kOutput, calls=%fused_computation.21 | convolution fusion | flops 3631349248 | bytes 14570496 | tf_op jit(solution)/shard_map/dot_general | solution.py:17
  96.8 16.3 %pmax.7 = f32[384]{0:T(512)S(1)} all-reduce(f32[384]{0:T(512)S(1)} %get-tuple-element.11), channel_id=1, replica_groups=mesh['dp'=32,'tensor'=8] {'tensor'}, use_global_device_ids=true, to_apply=%region_2.0 | all-reduce | flops 384 | bytes 3072 | tf_op jit(solution)/shard_map/pmax | solution.py:20
  113.2 1.8 exponential_reduce_fusion
  115.0 0.6 exponential_multiply_fusion
  115.5 16.5 %psum.21 = f32[384]{0:T(512)S(1)} all-reduce(f32[384]{0:T(512)} %exponential_multiply_fusion), channel_id=1, replica_groups=mesh['dp'=32,'tensor'=8] {'tensor'}, use_global_device_ids=true, to_apply=%region_4.0 | all-reduce | flops 384 | bytes 3072 | tf_op jit(solution)/shard_map/psum | solution.py:21
  132.0 0.6 copy-done.2
  132.6 11.1 %convolution_bitcast_fusion = f32[4608,384]{0,1:T(8,128)} fusion(bf16[4608,1024]{1,0:T(8,128)(2,1)} %param.6, f32[384,1024]{1,0:T(8,128)} %get-tuple-element.12, s32[1024]{0:T(1024)S(1)} %iota_add_fusion, f32[384]{0:T(512)S(1)} %log_add_fusion, s32[384]{0:T(512)} %param.7), kind=kOutput, calls=%fused_computation.2 | convolution fusion | flops 3625844736 | bytes 18095104 | tf_op jit(solution)/shard_map/dot_general | solution.py:31
  143.7 8.0 %copy.11 = f32[4608,384]{1,0:T(8,128)} copy(f32[4608,384]{0,1:T(8,128)} %convolution_bitcast_fusion) | data formatting | bytes 14155776
  152.0 0.4 copy-done.3
  152.4 11.5 %fusion.3 = f32[4608,1024]{1,0:T(8,128)} fusion(bf16[384,4608]{0,1:T(8,128)(2,1)S(1)} %copy-done, f32[4608]{0:T(1024)} %param.5, f32[384]{0:T(512)S(1)} %add_rsqrt_fusion, f32[384,1024]{1,0:T(8,128)} %get-tuple-element.12, s32[1024]{0:T(1024)S(1)} %iota_add_fusion, f32[384]{0:T(512)S(1)} %copy-done.3, s32[384]{0:T(512)S(1)} %copy-done.4), kind=kOutput, calls=%fused_computation.8 | convolution fusion | flops 3632922624 | bytes 24013312 | tf_op jit(solution)/shard_map/dot_general | solution.py:47
  163.9 1.0 copy-done.1
  164.9 0.3 copy.9
  165.2 0.8 dynamic_slice.3
  166.0 102.0 %reduce-scatter.7.cloned.1.call-done = f32[576,384]{1,0:T(8,128)} async-done(((f32[4608,384]{1,0:T(8,128)}), f32[576,384]{1,0:T(8,128)}) %reduce-scatter.7.cloned.1.call-update) | async-done | bytes 884752
  267.9 1.5 copy.12
  269.4 0.4 fusion.7
  269.9 16.1 %psum.22 = f32[384]{0:T(512)S(1)} all-reduce(f32[384]{0:T(512)S(1)} %get-tuple-element.10), channel_id=1, replica_groups=mesh['dp'=32,'tensor'=8] {'tensor'}, use_global_device_ids=true, to_apply=%region_7.0 | all-reduce | flops 384 | bytes 3072 | tf_op jit(solution)/shard_map/psum | solution.py:40
  285.9 0.2 subtract_multiply_fusion
  286.2 1.2 copy.10
  287.4 60.1 %psum.23 = f32[576]{0:T(1024)} all-reduce(f32[576]{0:T(1024)S(1)} %get-tuple-element.9), channel_id=1, replica_groups=mesh['dp'=32,'tensor'=8] {'dp'}, use_global_device_ids=true, to_apply=%region_10.0 | all-reduce | flops 576 | bytes 4608 | tf_op jit(solution)/shard_map/psum | solution.py:45
  347.5 67.5 %reduce-scatter.5.cloned.1.call-done = f32[144,1024]{1,0:T(8,128)} async-done(((f32[4608,1024]{1,0:T(8,128)}), f32[144,1024]{1,0:T(8,128)}) %reduce-scatter.5.cloned.1.call-update) | async-done | bytes 589840 | tf_op jit(solution)/shard_map/reduce_scatter | solution.py:46
  (16 shorter events, 0.4 us)
Async XLA Ops:
  7.2 77.8 %all-gather.2.cloned.1.call-start = ((), (), s32[]{:S(2)}) async-start(), calls=%async_computation.2 | async-start | bytes 3981312 | tf_op jit(solution)/shard_map/all_gather | solution.py:13
  7.9 260.0 %reduce-scatter.7.cloned.1.call-start = ((), (), s32[]{:S(2)}) async-start(), calls=%async_computation.4 | async-start | bytes 7962624
  85.0 3.1 copy-start
  132.0 0.6 copy-start.2
  151.7 0.7 copy-start.3
  151.7 0.7 copy-start.4
  151.7 263.3 %reduce-scatter.5.cloned.1.call-start = ((), (), s32[]{:S(2)}) async-start(), calls=%async_computation.3 | async-start | bytes 19464192 | tf_op jit(solution)/shard_map/reduce_scatter | solution.py:46
  163.9 1.0 copy-start.1
Sparse Core Ops, SparseCore 0:
  10.6 74.3 all-gather.1
  151.9 116.0 reduce-scatter.6
  271.2 143.7 reduce-scatter.4
where the time goes:
time: 424 us; the launch traced here: 422 us
  waiting for transfers between devices  247 us (58%)
  blocking collectives  109 us (26%)
  matrix products  31.3 us (7%)
  local copies, waits for them, and re-layouts  13.9 us (3%)
  between operations  13.8 us (3%)
  other arithmetic  6.05 us (1%)
    unnamed x4, waiting for transfers between devices  103 us
    all_gather x1, waiting for transfers between devices, shards(): gathered = lax.all_gather(hidden_input_state, 'tensor', axis=1, tiled=True)  77 us
    reduce_scatter x1, waiting for transfers between devices, shards(): lax.psum_scatter(lax.dot_general(normed, dlogits, (((0,), (0,)), ((), ())...  67.5 us
    psum x1, blocking collectives, shards(): lax.psum(jnp.sum(normed_gradient * normalized_slice, axis=0), 'dp')  60.1 us
    psum x1, blocking collectives, shards(): row_total = lax.psum(local_total * jnp.exp(local_top - row_top), 'tensor')  16.5 us
    pmax x1, blocking collectives, shards(): row_top = lax.pmax(local_top, 'tensor')  16.3 us
    psum x1, blocking collectives, shards(): row_inner_sum = lax.psum(partial_inner_sum, 'tensor') / width  16.1 us
    unnamed x14, local copies, waits for them, and re-layouts  13.1 us
  transfers between devices with their start and end apart: 3, of which 3 were waited for; matrix products, arithmetic and copies ran while one was open for 4% of the time, Pallas kernels for 0%

commit v1 on v0

v1 whole, which is shorter than its diff:
```python
import jax
import jax.numpy as jnp
import numpy as np
from jax import lax
from jax.sharding import PartitionSpec as P

epsilon = 1e-06


def ring_order(n_hi, n_lo):
    order = []
    for hi in range(n_hi):
        los = range(n_lo) if hi % 2 == 0 else range(n_lo - 1, -1, -1)
        order += [hi * n_lo + lo for lo in los]
    return order


def ring_reduce_scatter(fwd, bwd, axis, order):
    n = len(order)
    pos_of = np.zeros(n, np.int32)
    for p, t in enumerate(order):
        pos_of[t] = p
    order_arr = jnp.asarray(np.asarray(order, np.int32))
    me = lax.axis_index(axis)
    pos = jnp.asarray(pos_of)[me]
    perm_f = [(order[p], order[(p + 1) % n]) for p in range(n)]
    perm_b = [(order[p], order[(p - 1) % n]) for p in range(n)]
    recv_f = recv_b = None
    for s in range(n - 1):
        qf = order_arr[(pos - 1 - s) % n]
        qb = order_arr[(pos + 1 + s) % n]
        send_f = lax.dynamic_index_in_dim(fwd, qf, 0, keepdims=False)
        send_b = lax.dynamic_index_in_dim(bwd, qb, 0, keepdims=False)
        if recv_f is not None:
            send_f = send_f + recv_f
            send_b = send_b + recv_b
        recv_f = lax.ppermute(send_f, axis, perm_f)
        recv_b = lax.ppermute(send_b, axis, perm_b)
    own_f = lax.dynamic_index_in_dim(fwd, me, 0, keepdims=False)
    own_b = lax.dynamic_index_in_dim(bwd, me, 0, keepdims=False)
    return own_f + recv_f, own_b + recv_b


def shards(hidden_input_state, norm_gain, head_weight, target_ids):
    tokens, local_cols = hidden_input_state.shape
    width, vocab_rows = head_weight.shape
    n_tensor = width // local_cols
    gathered = lax.all_gather(hidden_input_state, "tensor", axis=1, tiled=True)
    values = gathered.astype(jnp.float32)
    scaled_rows = lax.rsqrt(jnp.mean(values * values, axis=1, keepdims=True) + epsilon)
    normalized = values * scaled_rows
    normed = (normalized * norm_gain[None, :]).astype(jnp.bfloat16)
    logits = jnp.dot(normed, head_weight, preferred_element_type=jnp.float32)
    local_top = jnp.max(logits, axis=1)
    local_total = jnp.sum(jnp.exp(logits - local_top[:, None]), axis=1)
    stats = lax.all_gather(jnp.stack([local_top, local_total]), "tensor", axis=0)
    row_top = jnp.max(stats[:, 0, :], axis=0)
    row_total = jnp.sum(stats[:, 1, :] * jnp.exp(stats[:, 0, :] - row_top[None, :]), axis=0)
    log_total = row_top + jnp.log(row_total)
    offset = lax.axis_index("tensor") * vocab_rows
    column_ids = offset + lax.broadcasted_iota(jnp.int32, (1, vocab_rows), 1)
    onehot = (column_ids == target_ids[:, None]).astype(jnp.float32)
    dlogits = (jnp.exp(logits - log_total[:, None]) - onehot).astype(jnp.bfloat16)

    grad_head = lax.psum_scatter(
        lax.dot_general(
            normed, dlogits, (((0,), (0,)), ((), ())), preferred_element_type=jnp.float32
        ),
        "dp",
        scatter_dimension=0,
        tiled=True,
    )

    partial = lax.dot_general(
        head_weight, dlogits, (((1,), (1,)), ((), ())), preferred_element_type=jnp.float32
    )
    inner_part = jnp.sum(partial * (norm_gain[:, None] * normalized.T), axis=0)
    chunks = partial.reshape(n_tensor, local_cols, tokens)
    half = local_cols // 2
    extra = jnp.zeros((n_tensor, 8, tokens), jnp.float32).at[:, 0, :].set(
        jnp.broadcast_to(inner_part[None, :], (n_tensor, tokens))
    )
    fwd = jnp.concatenate([chunks[:, :half, :], extra], axis=1)
    bwd = chunks[:, half:, :]
    order = ring_order(2, n_tensor // 2)
    got_f, got_b = ring_reduce_scatter(fwd, bwd, "tensor", order)
    grad_cols = jnp.concatenate([got_f[:half], got_b], axis=0)
    row_inner_sum = got_f[half] / width

    normed_gradient = grad_cols.T
    start_col = lax.axis_index("tensor") * local_cols
    normalized_slice = hidden_input_state.astype(jnp.float32) * scaled_rows
    gain_slice = lax.dynamic_slice_in_dim(norm_gain, start_col, local_cols)
    weighted_rows = normed_gradient * gain_slice[None, :]
    hidden_state_gradient = scaled_rows * (
        weighted_rows - normalized_slice * row_inner_sum[:, None]
    )
    norm_gain_gradient = lax.psum(jnp.sum(normed_gradient * normalized_slice, axis=0), "dp")
    return (hidden_state_gradient, grad_head, norm_gain_gradient)


def solution(mesh):
    return jax.shard_map(
        shards,
        mesh=mesh,
        in_specs=(P("dp", "tensor"), P(), P(None, "tensor"), P("dp")),
        out_specs=(P("dp", "tensor"), P("dp", "tensor"), P("tensor")),
        check_vma=False,
    )
```

time: 424 us -> 410 us (0.967)
  waiting for transfers between devices: 247 us -> 161 us
  between operations: 13.8 us -> 50.1 us
  starting transfers between devices: 0.3 us -> 29.3 us
  other arithmetic: 6.05 us -> 28.1 us
  blocking collectives: 109 us -> 89.8 us
  local copies, waits for them, and re-layouts: 13.9 us -> 22.9 us
    unnamed x4 -> x2, waiting for transfers between devices: 103 us -> 0.7 us
    ppermute x0 -> x14, waiting for transfers between devices: none -> 83.3 us  [the longest x7 55.6 us: ring_reduce_scatter(): recv_b = lax.ppermute(send_b, axis, perm_b)]
    reduce_scatter x1, waiting for transfers between devices: 67.5 us -> 0.01 us  [shards(): lax.psum_scatter(lax.dot_general(normed, dlogits, (((0,), (0,)), ((), ())...]
    psum x2 -> x0, blocking collectives: 32.5 us -> none  [the longest x1 16.5 us: shards(): row_total = lax.psum(local_total * jnp.exp(local_top - row_top), 'tensor')]
    ppermute x0 -> x14, starting transfers between devices: none -> 29.2 us  [the longest x7 28.5 us: ring_reduce_scatter(): recv_b = lax.ppermute(send_b, axis, perm_b)]
    all_gather x0 -> x1, blocking collectives: none -> 27.8 us  [shards(): lax.all_gather(jnp.stack([local_top, local_total]), 'tensor', axis=0)]
    add x0 -> x14, other arithmetic: none -> 25.4 us  [the longest x6 11.8 us: ring_reduce_scatter(): send_f = send_f + recv_f]
    pmax x1 -> x0, blocking collectives: 16.3 us -> none  [shards(): row_top = lax.pmax(local_top, 'tensor')]
  transfers between devices with their start and end apart: 3 -> 16, of which waited for: 3 -> 12; matrix products, arithmetic and copies ran while one was open for 4% -> 13% of each run, Pallas kernels for 0% -> 0%
where the time goes in v1:
time: 410 us; the launch traced here: 409 us
  waiting for transfers between devices  161 us (39%)
  blocking collectives  89.8 us (22%)
  between operations  50.1 us (12%)
  starting transfers between devices  29.3 us (7%)
  other arithmetic  28.1 us (7%)
  matrix products  27.6 us (7%)
  local copies, waits for them, and re-layouts  22.9 us (6%)
    all_gather x1, waiting for transfers between devices, shards(): gathered = lax.all_gather(hidden_input_state, 'tensor', axis=1, tiled=True)  77 us
    psum x1, blocking collectives, shards(): lax.psum(jnp.sum(normed_gradient * normalized_slice, axis=0), 'dp')  62 us
    ppermute x7, waiting for transfers between devices, ring_reduce_scatter(): recv_b = lax.ppermute(send_b, axis, perm_b)  55.6 us
    ppermute x7, starting transfers between devices, ring_reduce_scatter(): recv_b = lax.ppermute(send_b, axis, perm_b)  28.5 us
    all_gather x1, blocking collectives, shards(): lax.all_gather(jnp.stack([local_top, local_total]), 'tensor', axis=0)  27.8 us
    ppermute x7, waiting for transfers between devices, ring_reduce_scatter(): recv_f = lax.ppermute(send_f, axis, perm_f)  27.7 us
    add x6, other arithmetic, ring_reduce_scatter(): send_f = send_f + recv_f  11.8 us
    dot_general x1, matrix products, shards(): lax.dot_general(head_weight, dlogits, (((1,), (1,)), ((), ())), preferred...  11.5 us
  transfers between devices with their start and end apart: 16, of which 12 were waited for; matrix products, arithmetic and copies ran while one was open for 13% of the time, Pallas kernels for 0%

profile of v1, /device:TPU:1, one launch (start us, length us, event | category | flops | bytes accessed | tf_op | source)
XLA Modules:
  0.0 408.9 jit_solution(1212143429641370767)
XLA Ops:
  8.0 77.0 %all-gather.4.cloned.1.call-done = bf16[384,4608]{0,1:T(8,128)(2,1)} async-done(((bf16[384,576]{0,1:T(8,128)(2,1)}), bf16[384,4608]{0,1:T(8,128)(2,1)}) %all-gather.4.cloned.1.call-update) | async-done | bytes 3538960 | tf_op jit(solution)/shard_map/all_gather | solution.py:48
  85.0 4.3 %copy.30 = bf16[384,4608]{1,0:T(8,128)(2,1)S(1)} copy(bf16[384,4608]{0,1:T(8,128)(2,1)} %all-gather.4.cloned.1.call-done) | data formatting | bytes 7077888 | tf_op jit(solution)/shard_map/all_gather | solution.py:48
  90.1 6.6 %fusion.17 = (f32[384]{0:T(512)S(1)}, f32[384,1024]{1,0:T(8,128)S(1)}) fusion(bf16[4608,1024]{1,0:T(8,128)(2,1)} %param.10, bf16[384,4608]{1,0:T(8,128)(2,1)S(1)} %copy.30, f32[4608]{0:T(1024)S(1)} %copy-done.6, f32[384]{0:T(512)S(1)} %add_rsqrt_fusion), kind=kOutput, calls=%fused_computation.50 | convolution fusion | flops 3631349248 | bytes 14570496 | tf_op jit(solution)/shard_map/dot_general | solution.py:53
  97.2 27.8 %all-gather.1 = f32[8,2,384]{2,1,0:T(2,128)S(1)} all-gather(f32[1,2,384]{2,1,0:T(2,128)S(1)} %maximum_bitcast_fusion.1), channel_id=2, replica_groups=mesh['dp'=32,'tensor'=8] {'tensor'}, dimensions={0}, use_global_device_ids=true | all-gather | bytes 27648 | tf_op jit(solution)/shard_map/all_gather | solution.py:56
  125.1 9.5 %fusion.6 = f32[4608,1024]{1,0:T(8,128)} fusion(bf16[384,4608]{1,0:T(8,128)(2,1)S(1)} %copy.30, f32[4608]{0:T(1024)S(1)} %copy-done.6, f32[384]{0:T(512)S(1)} %add_rsqrt_fusion, f32[384,1024]{1,0:T(8,128)S(1)} %get-tuple-element.37, s32[1024]{0:T(1024)S(1)} %iota_add_fusion, f32[384]{0:T(512)S(1)} %log_add_fusion, s32[384]{0:T(512)S(1)} %copy-done.7), kind=kOutput, calls=%fused_computation.13 | convolution fusion | flops 3632922624 | bytes 24013312 | tf_op jit(solution)/shard_map/dot_general | solution.py:66
  149.5 11.5 %fusion.5 = (f32[384]{0:T(512)S(1)}, f32[4608,384]{0,1:T(8,128)}) fusion(bf16[384,4608]{1,0:T(8,128)(2,1)S(1)} %copy.30, f32[4608]{0:T(1024)} %param.9, f32[384]{0:T(512)S(1)} %add_rsqrt_fusion, bf16[4608,1024]{1,0:T(8,128)(2,1)} %param.10, f32[384,1024]{1,0:T(8,128)} %copy-done.3, s32[1024]{0:T(1024)S(1)} %iota_add_fusion, f32[384]{0:T(512)S(1)} %log_add_fusion, ...), kind=kOutput, calls=%fused_computation.8 | convolution fusion | flops 3634691584 | bytes 21655552 | tf_op jit(solution)/shard_map/dot_general | solution.py:74
  161.0 8.1 %copy.32 = f32[4608,384]{1,0:T(8,128)} copy(f32[4608,384]{0,1:T(8,128)} %get-tuple-element.39) | data formatting | bytes 14155776 | tf_op jit(solution)/shard_map/dot_general | solution.py:74
  169.1 3.7 fusion.14
  182.4 16.3 %collective-permute-done.7 = f32[288,384]{1,0:T(8,128)} collective-permute-done((f32[288,384]{1,0:T(8,128)}, f32[288,384]{1,0:T(8,128)}, u32[]{:S(2)}, u32[]{:S(2)}) %collective-permute-start.7) | collective-permute-done | bytes 442400 | tf_op jit(solution)/shard_map/ppermute | solution.py:38
  200.7 7.0 %collective-permute-start.8 = (f32[288,384]{1,0:T(8,128)}, f32[288,384]{1,0:T(8,128)}, u32[]{:S(2)}, u32[]{:S(2)}) collective-permute-start(f32[288,384]{1,0:T(8,128)} %bitcast_add_fusion.7), channel_id=1, source_target_pairs={{0,4},{1,0},{2,1},{3,2},{7,3},{6,7},{5,6},{4,5},{8,12},{9,8},{10,9... | collective-permute-start | bytes 1327112 | tf_op jit(solution)/shard_map/ppermute | solution.py:38
  207.7 7.3 %collective-permute-done = f32[296,384]{1,0:T(8,128)} collective-permute-done((f32[296,384]{1,0:T(8,128)}, f32[296,384]{1,0:T(8,128)}, u32[]{:S(2)}, u32[]{:S(2)}) %collective-permute-start) | collective-permute-done | bytes 454688 | tf_op jit(solution)/shard_map/ppermute | solution.py:37
  220.7 10.4 %collective-permute-done.8 = f32[288,384]{1,0:T(8,128)} collective-permute-done((f32[288,384]{1,0:T(8,128)}, f32[288,384]{1,0:T(8,128)}, u32[]{:S(2)}, u32[]{:S(2)}) %collective-permute-start.8) | collective-permute-done | bytes 442400 | tf_op jit(solution)/shard_map/ppermute | solution.py:38
  233.1 6.2 %collective-permute-start.9 = (f32[288,384]{1,0:T(8,128)}, f32[288,384]{1,0:T(8,128)}, u32[]{:S(2)}, u32[]{:S(2)}) collective-permute-start(f32[288,384]{1,0:T(8,128)} %bitcast_add_fusion.8), channel_id=1, source_target_pairs={{0,4},{1,0},{2,1},{3,2},{7,3},{6,7},{5,6},{4,5},{8,12},{9,8},{10,9... | collective-permute-start | bytes 1327112 | tf_op jit(solution)/shard_map/ppermute | solution.py:38
  239.3 10.3 %collective-permute-done.1 = f32[296,384]{1,0:T(8,128)} collective-permute-done((f32[296,384]{1,0:T(8,128)}, f32[296,384]{1,0:T(8,128)}, u32[]{:S(2)}, u32[]{:S(2)}) %collective-permute-start.1) | collective-permute-done | bytes 454688 | tf_op jit(solution)/shard_map/ppermute | solution.py:37
  255.1 18.2 %collective-permute-done.9 = f32[288,384]{1,0:T(8,128)} collective-permute-done((f32[288,384]{1,0:T(8,128)}, f32[288,384]{1,0:T(8,128)}, u32[]{:S(2)}, u32[]{:S(2)}) %collective-permute-start.9) | collective-permute-done | bytes 442400 | tf_op jit(solution)/shard_map/ppermute | solution.py:38
  275.2 3.8 collective-permute-start.10
  279.0 5.7 %collective-permute-done.2 = f32[296,384]{1,0:T(8,128)} collective-permute-done((f32[296,384]{1,0:T(8,128)}, f32[296,384]{1,0:T(8,128)}, u32[]{:S(2)}, u32[]{:S(2)}) %collective-permute-start.2) | collective-permute-done | bytes 454688 | tf_op jit(solution)/shard_map/ppermute | solution.py:37
  290.6 3.5 collective-permute-done.10
  295.9 3.7 collective-permute-start.11
  309.5 3.7 collective-permute-start.12
  322.2 3.7 collective-permute-start.13
  328.7 3.4 collective-permute-done.13
  333.1 4.5 %collective-permute-done.6 = f32[296,384]{1,0:T(8,128)} collective-permute-done((f32[296,384]{1,0:T(8,128)}, f32[296,384]{1,0:T(8,128)}, u32[]{:S(2)}, u32[]{:S(2)}) %collective-permute-start.6) | collective-permute-done | bytes 454688 | tf_op jit(solution)/shard_map/ppermute | solution.py:37
  340.0 62.0 %psum.7 = f32[576]{0:T(1024)} all-reduce(f32[576]{0:T(1024)S(1)} %get-tuple-element.17), channel_id=1, replica_groups=mesh['dp'=32,'tensor'=8] {'dp'}, use_global_device_ids=true, to_apply=%region_8.9 | all-reduce | flops 576 | bytes 4608 | tf_op jit(solution)/shard_map/psum | solution.py:98
  (68 shorter events, 40.5 us)
Async XLA Ops:
  7.2 77.8 %all-gather.4.cloned.1.call-start = ((), (), s32[]{:S(2)}) async-start(), calls=%async_computation.1 | async-start | bytes 3981312 | tf_op jit(solution)/shard_map/all_gather | solution.py:48
  7.9 394.1 %reduce-scatter.2.cloned.1.call-start = ((), (), s32[]{:S(2)}) async-start(), calls=%async_computation.2 | async-start | bytes 19464192 | tf_op jit(solution)/shard_map/reduce_scatter | solution.py:65
  89.3 0.8 copy-start.6
  90.1 35.0 %copy-start.7 = (s32[384]{0:T(512)S(1)}, s32[384]{0:T(512)}, u32[]{:S(2)}) copy-start(s32[384]{0:T(512)} %param.11) | copy-start | bytes 4612
  96.8 28.3 %copy-start.3 = (f32[384,1024]{1,0:T(8,128)}, f32[384,1024]{1,0:T(8,128)S(1)}, u32[]{:S(2)}) copy-start(f32[384,1024]{1,0:T(8,128)S(1)} %get-tuple-element.37) | copy-start | bytes 4718596
  134.6 0.7 copy-start.5
  172.8 1.9 copy-start.1
  173.7 25.0 %collective-permute-start.7 = (f32[288,384]{1,0:T(8,128)}, f32[288,384]{1,0:T(8,128)}, u32[]{:S(2)}, u32[]{:S(2)}) collective-permute-start(f32[288,384]{1,0:T(8,128)} %dynamic-slice_bitcast_fusion.1), channel_id=1, source_target_pairs={{0,4},{1,0},{2,1},{3,2},{7,3},{6,7},{5,6},{4,5},{8,12},{9,8},{10,9... | collective-permute-start | bytes 1327112 | tf_op jit(solution)/shard_map/ppermute | solution.py:38
  174.7 1.9 copy-start
  177.4 96.0 %copy-start.2 = (f32[8,288,384]{2,1,0:T(8,128)S(1)}, f32[8,288,384]{2,1,0:T(8,128)}, u32[]{:S(2)}) copy-start(f32[8,288,384]{2,1,0:T(8,128)} %copy-done.1) | copy-start | bytes 10616836
  177.4 37.6 %collective-permute-start = (f32[296,384]{1,0:T(8,128)}, f32[296,384]{1,0:T(8,128)}, u32[]{:S(2)}, u32[]{:S(2)}) collective-permute-start(f32[296,384]{1,0:T(8,128)} %dynamic-slice_bitcast_fusion), channel_id=1, source_target_pairs={{0,1},{1,2},{2,3},{3,7},{7,6},{6,5},{5,4},{4,0},{8,9},{9,10},{10,1... | collective-permute-start | bytes 1363976 | tf_op jit(solution)/shard_map/ppermute | solution.py:37
  200.7 30.4 %collective-permute-start.8 = (f32[288,384]{1,0:T(8,128)}, f32[288,384]{1,0:T(8,128)}, u32[]{:S(2)}, u32[]{:S(2)}) collective-permute-start(f32[288,384]{1,0:T(8,128)} %bitcast_add_fusion.7), channel_id=1, source_target_pairs={{0,4},{1,0},{2,1},{3,2},{7,3},{6,7},{5,6},{4,5},{8,12},{9,8},{10,9... | collective-permute-start | bytes 1327112 | tf_op jit(solution)/shard_map/ppermute | solution.py:38
  217.0 32.6 %collective-permute-start.1 = (f32[296,384]{1,0:T(8,128)}, f32[296,384]{1,0:T(8,128)}, u32[]{:S(2)}, u32[]{:S(2)}) collective-permute-start(f32[296,384]{1,0:T(8,128)} %bitcast_add_fusion), channel_id=1, source_target_pairs={{0,1},{1,2},{2,3},{3,7},{7,6},{6,5},{5,4},{4,0},{8,9},{9,10},{10,1... | collective-permute-start | bytes 1363976 | tf_op jit(solution)/shard_map/ppermute | solution.py:37
  233.1 40.3 %collective-permute-start.9 = (f32[288,384]{1,0:T(8,128)}, f32[288,384]{1,0:T(8,128)}, u32[]{:S(2)}, u32[]{:S(2)}) collective-permute-start(f32[288,384]{1,0:T(8,128)} %bitcast_add_fusion.8), channel_id=1, source_target_pairs={{0,4},{1,0},{2,1},{3,2},{7,3},{6,7},{5,6},{4,5},{8,12},{9,8},{10,9... | collective-permute-start | bytes 1327112 | tf_op jit(solution)/shard_map/ppermute | solution.py:38
  251.6 33.1 %collective-permute-start.2 = (f32[296,384]{1,0:T(8,128)}, f32[296,384]{1,0:T(8,128)}, u32[]{:S(2)}, u32[]{:S(2)}) collective-permute-start(f32[296,384]{1,0:T(8,128)} %bitcast_add_fusion.1), channel_id=1, source_target_pairs={{0,1},{1,2},{2,3},{3,7},{7,6},{6,5},{5,4},{4,0},{8,9},{9,10},{10,1... | collective-permute-start | bytes 1363976 | tf_op jit(solution)/shard_map/ppermute | solution.py:37
  275.2 18.9 %collective-permute-start.10 = (f32[288,384]{1,0:T(8,128)}, f32[288,384]{1,0:T(8,128)}, u32[]{:S(2)}, u32[]{:S(2)}) collective-permute-start(f32[288,384]{1,0:T(8,128)} %bitcast_add_fusion.9), channel_id=1, source_target_pairs={{0,4},{1,0},{2,1},{3,2},{7,3},{6,7},{5,6},{4,5},{8,12},{9,8},{10,9... | collective-permute-start | bytes 1327112 | tf_op jit(solution)/shard_map/ppermute | solution.py:38
  286.7 13.0 %collective-permute-start.3 = (f32[296,384]{1,0:T(8,128)}, f32[296,384]{1,0:T(8,128)}, u32[]{:S(2)}, u32[]{:S(2)}) collective-permute-start(f32[296,384]{1,0:T(8,128)} %bitcast_add_fusion.2), channel_id=1, source_target_pairs={{0,1},{1,2},{2,3},{3,7},{7,6},{6,5},{5,4},{4,0},{8,9},{9,10},{10,1... | collective-permute-start | bytes 1363976 | tf_op jit(solution)/shard_map/ppermute | solution.py:37
  295.9 11.7 %collective-permute-start.11 = (f32[288,384]{1,0:T(8,128)}, f32[288,384]{1,0:T(8,128)}, u32[]{:S(2)}, u32[]{:S(2)}) collective-permute-start(f32[288,384]{1,0:T(8,128)} %bitcast_add_fusion.10), channel_id=1, source_target_pairs={{0,4},{1,0},{2,1},{3,2},{7,3},{6,7},{5,6},{4,5},{8,12},{9,8},{10,9... | collective-permute-start | bytes 1327112 | tf_op jit(solution)/shard_map/ppermute | solution.py:38
  301.6 11.6 %collective-permute-start.4 = (f32[296,384]{1,0:T(8,128)}, f32[296,384]{1,0:T(8,128)}, u32[]{:S(2)}, u32[]{:S(2)}) collective-permute-start(f32[296,384]{1,0:T(8,128)} %bitcast_add_fusion.3), channel_id=1, source_target_pairs={{0,1},{1,2},{2,3},{3,7},{7,6},{6,5},{5,4},{4,0},{8,9},{9,10},{10,1... | collective-permute-start | bytes 1363976 | tf_op jit(solution)/shard_map/ppermute | solution.py:37
  309.5 10.8 %collective-permute-start.12 = (f32[288,384]{1,0:T(8,128)}, f32[288,384]{1,0:T(8,128)}, u32[]{:S(2)}, u32[]{:S(2)}) collective-permute-start(f32[288,384]{1,0:T(8,128)} %bitcast_add_fusion.11), channel_id=1, source_target_pairs={{0,4},{1,0},{2,1},{3,2},{7,3},{6,7},{5,6},{4,5},{8,12},{9,8},{10,9... | collective-permute-start | bytes 1327112 | tf_op jit(solution)/shard_map/ppermute | solution.py:38
  315.2 10.7 %collective-permute-start.5 = (f32[296,384]{1,0:T(8,128)}, f32[296,384]{1,0:T(8,128)}, u32[]{:S(2)}, u32[]{:S(2)}) collective-permute-start(f32[296,384]{1,0:T(8,128)} %bitcast_add_fusion.4), channel_id=1, source_target_pairs={{0,1},{1,2},{2,3},{3,7},{7,6},{6,5},{5,4},{4,0},{8,9},{9,10},{10,1... | collective-permute-start | bytes 1363976 | tf_op jit(solution)/shard_map/ppermute | solution.py:37
  322.2 9.9 %collective-permute-start.13 = (f32[288,384]{1,0:T(8,128)}, f32[288,384]{1,0:T(8,128)}, u32[]{:S(2)}, u32[]{:S(2)}) collective-permute-start(f32[288,384]{1,0:T(8,128)} %bitcast_add_fusion.12), channel_id=1, source_target_pairs={{0,4},{1,0},{2,1},{3,2},{7,3},{6,7},{5,6},{4,5},{8,12},{9,8},{10,9... | collective-permute-start | bytes 1327112 | tf_op jit(solution)/shard_map/ppermute | solution.py:38
  327.8 9.8 %collective-permute-start.6 = (f32[296,384]{1,0:T(8,128)}, f32[296,384]{1,0:T(8,128)}, u32[]{:S(2)}, u32[]{:S(2)}) collective-permute-start(f32[296,384]{1,0:T(8,128)} %bitcast_add_fusion.5), channel_id=1, source_target_pairs={{0,1},{1,2},{2,3},{3,7},{7,6},{6,5},{5,4},{4,0},{8,9},{9,10},{10,1... | collective-permute-start | bytes 1363976 | tf_op jit(solution)/shard_map/ppermute | solution.py:37
  327.8 11.0 %copy-start.4 = (bf16[384,576]{0,1:T(8,128)(2,1)S(1)}, bf16[384,576]{0,1:T(8,128)(2,1)}, u32[]{:S(2)}) copy-start(bf16[384,576]{0,1:T(8,128)(2,1)} %param.8) | copy-start | bytes 1327108
Sparse Core Ops, SparseCore 0:
  10.6 74.3 all-gather.3
  134.7 149.8 reduce-scatter.1
